TPU v7x, 32 devices: a whole 2x2x4 slice. The times are simulated.
32 devices in a mesh: freq: 4 (over y, core), row: 8 (over z, x).
Axes of the slice: x: 2, y: 2, z: 4, core: 2. Of those that a mesh axis runs over, the one named last changes fastest.
Arguments:
- traces: bfloat16 [2, 8192, 8192], P(None, ('freq', 'row')), may hold values from -1.1953125 to 1.1953125
- prior: bfloat16 [4, 2, 8192, 8192], P('freq', None, None, 'row'), may hold values from -0.796875 to 0.796875
- bins: int32 [4], replicated, may hold values from 64 to 255
- panels: int32 [2], replicated, may hold values from 0 to 31
Outputs:
- multiples: bfloat16 [4, 2, 8192, 8192], P('freq', None, 'row')
- spectrum: bfloat16 [4, 2, 8192, 8192], P('freq', None, None, 'row')
All inputs are finite; a program needn't handle non-finite values.
Results may differ from a plain program's by a relative error of at most 0.0077.
Values may be sent and summed in bfloat16 or wider, within the bound.
No kernel may reach another device: no remote copies, remote signals or barrier semaphores. Data moves between devices by JAX's collectives and lax.ppermute only.
A program may use at most 640 MiB of HBM per device.

v0:
```python
import math
import jax
import jax.numpy as jnp
from jax import lax
from jax.sharding import PartitionSpec as P

NT_REC = 1024
PANEL = 256
STEPS = 2
BLOCK_START = 1022


def spread(value, axis, source):
    kept = jnp.where(lax.axis_index(axis) == source, value, 0).astype(value.dtype)
    return lax.psum(kept, axis)


def complex_terms(left, right):
    dims = (((0,), (1,)), ((), ()))

    def product(first, second):
        return lax.dot_general(first, second, dims, preferred_element_type=jnp.float32)

    real_part = product(left[0], right[0]) - product(left[1], right[1])
    imag_part = product(left[0], right[1]) + product(left[1], right[0])
    return (real_part, imag_part)


def body(traces, prior, bins, panels):
    sample_count, shots_local, receivers = traces.shape
    row_count = lax.axis_size("row")
    block_rows = receivers // row_count
    sample_index = BLOCK_START + jnp.arange(sample_count, dtype=jnp.int32)
    turn_count = bins[:, None] * sample_index[None, :] % NT_REC
    angles = 2.0 * math.pi / NT_REC * turn_count.astype(jnp.float32)
    twiddle = jnp.stack([jnp.cos(angles), -jnp.sin(angles)], axis=1).astype(jnp.bfloat16)
    own_twiddle = lax.dynamic_index_in_dim(twiddle, lax.axis_index("freq"), 0, keepdims=False)
    by_row = lax.all_to_all(traces, "row", split_axis=2, concat_axis=1, tiled=True)
    gathered = lax.all_gather(by_row, "freq", axis=1, tiled=True)
    transformed = jnp.einsum(
        "tsb,ct->csb", gathered, own_twiddle, preferred_element_type=jnp.float32
    ).astype(jnp.bfloat16)
    spectrum = (prior[0].astype(jnp.float32) + transformed.astype(jnp.float32)).astype(jnp.bfloat16)
    panels_each = block_rows // PANEL
    real_sum = jnp.zeros((block_rows, receivers), jnp.float32)
    imag_sum = jnp.zeros((block_rows, receivers), jnp.float32)
    for panel_step in range(STEPS):
        chosen = panels[panel_step]
        owner = chosen // panels_each
        offset = chosen % panels_each * PANEL
        own_rows = lax.dynamic_slice_in_dim(spectrum, offset, PANEL, 2)
        panel_data = spread(own_rows, "row", owner)
        left = lax.dynamic_slice_in_dim(spectrum, chosen * PANEL, PANEL, 1)
        real_part, imag_part = complex_terms(left, panel_data)
        real_sum = real_sum + real_part
        imag_sum = imag_sum + imag_part
    return (jnp.stack([real_sum, imag_sum])[None].astype(jnp.bfloat16), spectrum[None])


def solution(mesh):
    return jax.shard_map(
        body,
        mesh=mesh,
        in_specs=(P(None, ("freq", "row"), None), P("freq", None, None, "row"), P(), P()),
        out_specs=(P("freq", None, "row", None), P("freq", None, None, "row")),
        check_vma=False,
    )
```

profile of v0, /device:TPU:0, one launch (start us, length us, event | category | flops | bytes accessed | tf_op | source)
XLA Modules:
  0.0 1370.1 jit_solution(301745803882222178)
XLA Ops:
  7.2 21.0 %copy.21 = bf16[2,256,8192]{1,0,2:T(2,128)(2,1)} copy(bf16[2,256,8192]{2,1,0:T(8,128)(2,1)} %param.4) | data formatting | bytes 16777216 | tf_op args[0]
  28.2 190.4 %all_to_all.18 = bf16[2,256,8192]{1,0,2:T(2,128)(2,1)} all-to-all(bf16[2,256,8192]{1,0,2:T(2,128)(2,1)} %copy.21), channel_id=1, replica_groups=mesh['freq'=4,'row'=8] {'row'}, dimensions={2} | all-to-all | bytes 16777216 | tf_op jit(solution)/shard_map/all_to_all | solution.py:38
  218.6 30.5 %copy.22 = bf16[2,8,256,1024]{3,0,2,1:T(2,128)(2,1)} copy(bf16[2,8,256,1024]{2,0,3,1:T(2,128)(2,1)} %bitcast.60) | data formatting | bytes 16777216 | tf_op jit(solution)/shard_map/all_to_all | solution.py:38
  249.1 0.0 all-reduce.3.cloned.1.call-start
  249.2 0.6 copy-done.1
  249.8 0.6 fusion.49
  255.3 0.1 cosine_convert_fusion
  255.4 0.2 fusion.45
  255.6 194.4 %all-gather.2.cloned.1.call-done = bf16[2,8192,1024]{2,0,1:T(2,128)(2,1)} async-done(((bf16[2,2048,1024]{2,0,1:T(2,128)(2,1)}), bf16[2,8192,1024]{2,0,1:T(2,128)(2,1)}) %all-gather.2.cloned.1.call-update) | async-done | bytes 33554448 | tf_op jit(solution)/shard_map/all_gather | solution.py:39
  449.9 145.3 %fusion = bf16[2,8192,1024]{2,0,1:T(2,128)(2,1)} fusion(bf16[1,2,8192,1024]{3,2,1,0:T(8,128)(2,1)} %param.5, bf16[2,8192,1024]{2,0,1:T(2,128)(2,1)} %all-gather.2.cloned.1.call-done, bf16[2,2]{1,0:T(2,128)(2,1)S(1)} %fusion.45), kind=kOutput, calls=%fused_computation.1 | convolution fusion | flops 150994944 | bytes 100663304 | tf_op jit(solution)/shard_map/tsb,ct->csb/dot_general | solution.py:40
  595.3 17.1 %broadcast_select_fusion.1 = (bf16[2,8192,256]{2,0,1:T(2,128)(2,1)}, bf16[2,8192,256]{2,0,1:T(2,128)(2,1)}) fusion(pred[]{:T(512)S(6)} %eq.11, bf16[2,8192,1024]{2,0,1:T(2,128)(2,1)} %fusion, s32[]{:T(128)S(6)} %select_n.71, s32[]{:T(128)S(6)} %select_n.77, pred[]{:T(512)S(6)} %eq.12), kind=kLoop, calls=%fused_computation.7 | loop fusion | flops 8388608 | bytes 33554440 | tf_op jit(solution)/shard_map/jit(_where)/select_n | solution.py:14
  613.6 23.4 %copy.23 = bf16[1,2,8192,1024]{3,2,1,0:T(8,128)(2,1)} copy(bf16[1,2,8192,1024]{3,1,2,0:T(2,128)(2,1)} %bitcast.58) | data formatting | bytes 67108864
  637.0 6.3 constant_dynamic-slice_fusion.3
  643.3 479.6 %all-reduce.3.cloned.1.call-done = (bf16[2,8192,256]{2,0,1:T(2,128)(2,1)}, bf16[2,8192,256]{2,0,1:T(2,128)(2,1)}) async-done(((bf16[2,8192,256]{2,0,1:T(2,128)(2,1)}, bf16[2,8192,256]{2,0,1:T(2,128)(2,1)}), (bf16[2,8192,256]{2,0,1:T(2,128)(2,1)}, bf16[2,8192,256]{2,0,1:T(2,128)(2,1)})) %all-reduce.3.cloned.1.call-update) | async-done | bytes 16777232 | tf_op jit(solution)/shard_map/psum | solution.py:15
  1122.9 33.0 %fusion.47 = (bf16[1,8192,256]{2,0,1:T(2,128)(2,1)}, bf16[1,8192,256]{2,0,1:T(2,128)(2,1)}, bf16[1,8192,256]{2,0,1:T(2,128)(2,1)}, bf16[1,8192,256]{2,0,1:T(2,128)(2,1)}) fusion(bf16[2,8192,256]{2,0,1:T(2,128)(2,1)} %get-tuple-element.12, bf16[2,8192,256]{2,0,1:T(2,128)(2,1)} %get-tuple-element.13), kind=kLoop, calls=%fused_computation.67 | loop fusion | bytes 33554432 | tf_op jit(solution)/shard_map/slice | solution.py:24
  1155.9 19.5 %fusion.11 = f32[1024,8192]{1,0:T(8,128)} fusion(bf16[1,8192,256]{2,0,1:T(2,128)(2,1)} %get-tuple-element.28, bf16[1,256,1024]{2,0,1:T(2,128)(2,1)} %get-tuple-element.17), kind=kOutput, calls=%fused_computation.18 | convolution fusion | flops 4294967296 | bytes 38273024 | tf_op jit(solution)/shard_map/dot_general | solution.py:22
  1175.3 16.5 %fusion.13 = f32[1024,8192]{1,0:T(8,128)} fusion(bf16[1,8192,256]{2,0,1:T(2,128)(2,1)} %get-tuple-element.29, bf16[1,256,1024]{2,0,1:T(2,128)(2,1)S(1)} %copy-done), kind=kOutput, calls=%fused_computation.20 | convolution fusion | flops 4294967296 | bytes 38273024 | tf_op jit(solution)/shard_map/dot_general | solution.py:22
  1191.9 16.5 %fusion.15 = f32[1024,8192]{1,0:T(8,128)} fusion(bf16[1,8192,256]{2,0,1:T(2,128)(2,1)} %get-tuple-element.29, bf16[1,256,1024]{2,0,1:T(2,128)(2,1)S(1)} %get-tuple-element.16), kind=kOutput, calls=%fused_computation.22 | convolution fusion | flops 4294967296 | bytes 38273024 | tf_op jit(solution)/shard_map/dot_general | solution.py:22
  1208.4 16.5 %fusion.9 = f32[1024,8192]{1,0:T(8,128)} fusion(bf16[1,8192,256]{2,0,1:T(2,128)(2,1)} %get-tuple-element.28, bf16[1,256,1024]{2,0,1:T(2,128)(2,1)S(1)} %get-tuple-element.16), kind=kOutput, calls=%fused_computation.16 | convolution fusion | flops 4294967296 | bytes 38273024 | tf_op jit(solution)/shard_map/dot_general | solution.py:22
  1225.0 16.5 %fusion.7 = f32[1024,8192]{1,0:T(8,128)} fusion(bf16[1,8192,256]{2,0,1:T(2,128)(2,1)} %get-tuple-element.20, bf16[1,256,1024]{2,0,1:T(2,128)(2,1)S(1)} %get-tuple-element.15), kind=kOutput, calls=%fused_computation.14 | convolution fusion | flops 4294967296 | bytes 38273024 | tf_op jit(solution)/shard_map/dot_general | solution.py:22
  1241.5 17.5 %fusion.3 = f32[1024,8192]{1,0:T(8,128)} fusion(bf16[1,8192,256]{2,0,1:T(2,128)(2,1)} %get-tuple-element.21, bf16[1,256,1024]{2,0,1:T(2,128)(2,1)S(1)} %get-tuple-element.15), kind=kOutput, calls=%fused_computation.10 | convolution fusion | flops 4294967296 | bytes 38273024 | tf_op jit(solution)/shard_map/dot_general | solution.py:22
  1259.0 40.7 %fusion.1 = bf16[1,1,1024,8192]{3,2,1,0:T(8,128)(2,1)} fusion(f32[1024,8192]{1,0:T(8,128)} %fusion.7, f32[1024,8192]{1,0:T(8,128)} %fusion.15, f32[1024,8192]{1,0:T(8,128)} %fusion.11, bf16[1,8192,256]{2,0,1:T(2,128)(2,1)} %get-tuple-element.21, bf16[1,256,1024]{2,0,1:T(2,128)(2,1)S(1)} %get-tuple-element.14), kind=kOutput, calls=%fused_computation.8 | convolution fusion | flops 4328521728 | bytes 122159104 | tf_op jit(solution)/shard_map/dot_general | solution.py:22
  1299.7 40.6 %fusion.2 = bf16[1,1,1024,8192]{3,2,1,0:T(8,128)(2,1)} fusion(f32[1024,8192]{1,0:T(8,128)} %fusion.3, f32[1024,8192]{1,0:T(8,128)} %fusion.9, f32[1024,8192]{1,0:T(8,128)} %fusion.13, bf16[1,8192,256]{2,0,1:T(2,128)(2,1)} %get-tuple-element.20, bf16[1,256,1024]{2,0,1:T(2,128)(2,1)S(1)} %get-tuple-element.14), kind=kOutput, calls=%fused_computation.9 | convolution fusion | flops 4328521728 | bytes 122159104 | tf_op jit(solution)/shard_map/dot_general | solution.py:22
  1340.3 23.0 %pad_maximum_fusion = bf16[1,2,1024,8192]{3,2,1,0:T(8,128)(2,1)} fusion(bf16[1,1,1024,8192]{3,2,1,0:T(8,128)(2,1)} %fusion.2, bf16[1,1,1024,8192]{3,2,1,0:T(8,128)(2,1)} %fusion.1), kind=kLoop, calls=%fused_computation.3 | loop fusion | flops 16777216 | bytes 67108864 | tf_op jit(solution)/shard_map/stack | solution.py:57
  (9 shorter events, 0.1 us)
Async XLA Ops:
  7.2 442.8 %all-gather.2.cloned.1.call-start = ((), (), s32[]{:S(2)}) async-start(), calls=%async_computation.1 | async-start | bytes 41943040 | tf_op jit(solution)/shard_map/all_gather | solution.py:39
  249.1 0.7 copy-start.1
  249.1 6.2 copy-start.2
  249.1 873.8 %all-reduce.3.cloned.1.call-start = ((), (), s32[]{:S(2)}) async-start(), calls=%async_computation.2 | async-start | bytes 33554432 | tf_op jit(solution)/shard_map/psum | solution.py:15
  1155.9 19.5 %copy-start = (bf16[1,256,1024]{2,0,1:T(2,128)(2,1)S(1)}, bf16[1,256,1024]{2,0,1:T(2,128)(2,1)}, u32[]{:S(2)}) copy-start(bf16[1,256,1024]{2,0,1:T(2,128)(2,1)} %get-tuple-element.17) | copy-start | bytes 1572868
Sparse Core Ops, SparseCore 0:
  249.2 200.6 all-gather.1
  612.5 510.3 all-reduce.2
where the time goes:
time: 1370 us
  waiting for transfers between devices  674 us (49%)
  matrix products  330 us (24%)
  blocking collectives  190 us (14%)
  local copies, waits for them, and re-layouts  115 us (8%)
  other arithmetic  40.3 us (3%)
  between operations  20.2 us (1%)
    psum x1, waiting for transfers between devices, spread(): return lax.psum(kept, axis)  480 us
    all_gather x1, waiting for transfers between devices, body(): gathered = lax.all_gather(by_row, 'freq', axis=1, tiled=True)  194 us
    all_to_all x1, blocking collectives, body(): lax.all_to_all(traces, 'row', split_axis=2, concat_axis=1, tiled=True)  190 us
    dot_general x8, matrix products, product(): lax.dot_general(first, second, dims, preferred_element_type=jnp.float32)  184 us
    dot_general x1, matrix products, body(): jnp.einsum('tsb,ct->csb', gathered, own_twiddle, preferred_element_type=j...  145 us
    unnamed x8, local copies, waits for them, and re-layouts  45 us
    slice x2, local copies, waits for them, and re-layouts, complex_terms(): real_part = product(left[0], right[0]) - product(left[1], right[1])  39.3 us
    all_to_all x1, local copies, waits for them, and re-layouts, body(): lax.all_to_all(traces, 'row', split_axis=2, concat_axis=1, tiled=True)  30.5 us
  transfers between devices with their start and end apart: 2, of which 2 were waited for; matrix products, arithmetic and copies ran while one was open for 2% of the time, Pallas kernels for 0%

commit v1 on v0

--- a/solution.py
+++ b/solution.py
@@ -12,7 +12,7 @@
 
 def spread(value, axis, source):
     kept = jnp.where(lax.axis_index(axis) == source, value, 0).astype(value.dtype)
-    return lax.psum(kept, axis)
+    return jnp.sum(jax.lax.all_gather(kept, axis), 0)
 
 
 def complex_terms(left, right):

time: 1370 us -> 3360 us (2.45)
  waiting for transfers between devices: 674 us -> 2630 us
  other arithmetic: 40.3 us -> 94.8 us
    all_gather x0 -> x2, waiting for transfers between devices: none -> 2430 us  [spread(): return jnp.sum(jax.lax.all_gather(kept, axis), 0)]
    psum x1 -> x0, waiting for transfers between devices: 480 us -> none  [spread(): return lax.psum(kept, axis)]
    reduce_sum x0 -> x2, other arithmetic: none -> 54.5 us  [spread(): return jnp.sum(jax.lax.all_gather(kept, axis), 0)]
  transfers between devices with their start and end apart: 2 -> 3, of which waited for: 2 -> 3; matrix products, arithmetic and copies ran while one was open for 2% -> 3% of each run, Pallas kernels for 0% -> 0%
where the time goes in v1:
time: 3360 us; the launch traced here: 3350 us
  waiting for transfers between devices  2630 us (78%)
  matrix products  320 us (10%)
  blocking collectives  190 us (6%)
  local copies, waits for them, and re-layouts  97.7 us (3%)
  other arithmetic  94.8 us (3%)
    all_gather x2, waiting for transfers between devices, spread(): return jnp.sum(jax.lax.all_gather(kept, axis), 0)  2430 us
    all_gather x1, waiting for transfers between devices, body(): gathered = lax.all_gather(by_row, 'freq', axis=1, tiled=True)  195 us
    all_to_all x1, blocking collectives, body(): lax.all_to_all(traces, 'row', split_axis=2, concat_axis=1, tiled=True)  190 us
    dot_general x8, matrix products, product(): lax.dot_general(first, second, dims, preferred_element_type=jnp.float32)  175 us
    dot_general x1, matrix products, body(): jnp.einsum('tsb,ct->csb', gathered, own_twiddle, preferred_element_type=j...  145 us
  transfers between devices with their start and end apart: 3, of which 3 were waited for; matrix products, arithmetic and copies ran while one was open for 3% of the time, Pallas kernels for 0%

profile of v1, /device:TPU:0, one launch (start us, length us, event | category | flops | bytes accessed | tf_op | source)
XLA Modules:
  0.0 3351.6 jit_solution(6603935982501079159)
XLA Ops:
  7.2 21.0 copy.37
  28.2 190.4 %all_to_all.18 = bf16[2,256,8192]{1,0,2:T(2,128)(2,1)} all-to-all(bf16[2,256,8192]{1,0,2:T(2,128)(2,1)} %copy.37), channel_id=1, replica_groups=mesh['freq'=4,'row'=8] {'row'}, dimensions={2} | all-to-all | bytes 16777216 | tf_op jit(solution)/shard_map/all_to_all | solution.py:38
  218.6 30.5 copy.38
  249.2 0.6 fusion.31
  255.3 194.8 %all-gather.6.cloned.1.call-done = bf16[2,8192,1024]{2,0,1:T(2,128)(2,1)} async-done(((bf16[2,2048,1024]{2,0,1:T(2,128)(2,1)}), bf16[2,8192,1024]{2,0,1:T(2,128)(2,1)}) %all-gather.6.cloned.1.call-update) | async-done | bytes 33554448 | tf_op jit(solution)/shard_map/all_gather | solution.py:39
  450.1 145.3 %fusion = bf16[2,8192,1024]{2,0,1:T(2,128)(2,1)} fusion(bf16[1,2,8192,1024]{3,2,1,0:T(8,128)(2,1)} %param.5, bf16[2,8192,1024]{2,0,1:T(2,128)(2,1)} %all-gather.6.cloned.1.call-done, bf16[2,2]{1,0:T(2,128)(2,1)S(1)} %fusion.29), kind=kOutput, calls=%fused_computation.1 | convolution fusion | flops 150994944 | bytes 100663304 | tf_op jit(solution)/shard_map/tsb,ct->csb/dot_general | solution.py:40
  595.4 17.1 broadcast_select_fusion.1
  612.5 7.7 copy.41
  620.7 8.1 copy.39
  630.1 23.4 copy.43
  653.5 6.4 constant_dynamic-slice_fusion.3
  659.9 1227.3 %all-gather.10.cloned.1.call-done = bf16[16,8192,256]{2,1,0:T(8,128)(2,1)} async-done(((bf16[2,8192,256]{2,1,0:T(8,128)(2,1)}), bf16[16,8192,256]{2,1,0:T(8,128)(2,1)}) %all-gather.10.cloned.1.call-update) | async-done | bytes 67108880 | tf_op jit(solution)/shard_map/all_gather | solution.py:15
  1887.1 28.6 reduce_sum.25
  1915.8 18.9 fusion.8
  1934.7 15.6 fusion.7
  1950.3 1205.3 %all-gather.8.cloned.1.call-done = bf16[16,8192,256]{2,1,0:T(8,128)(2,1)} async-done(((bf16[2,8192,256]{2,1,0:T(8,128)(2,1)}), bf16[16,8192,256]{2,1,0:T(8,128)(2,1)}) %all-gather.8.cloned.1.call-update) | async-done | bytes 67108880 | tf_op jit(solution)/shard_map/all_gather | solution.py:15
  3155.6 25.8 reduce_sum.24
  3181.4 15.3 fusion.5
  3196.8 15.3 fusion.4
  3212.1 15.5 fusion.3
  3227.6 15.3 fusion.6
  3243.0 39.5 %fusion.2 = bf16[1,1,1024,8192]{3,2,1,0:T(8,128)(2,1)} fusion(f32[1024,8192]{1,0:T(8,128)} %fusion.8, f32[1024,8192]{1,0:T(8,128)} %fusion.5, f32[1024,8192]{1,0:T(8,128)} %fusion.3, bf16[2,8192,256]{2,1,0:T(8,128)(2,1)} %reduce_sum.25, bf16[1,256,1024]{2,0,1:T(2,128)(2,1)S(1)} %get-tuple-element.14), kind=kOutput, calls=%fused_computation.9 | convolution fusion | flops 4328521728 | bytes 122159104 | tf_op jit(solution)/shard_map/dot_general | solution.py:22
  3282.4 39.4 %fusion.1 = bf16[1,1,1024,8192]{3,2,1,0:T(8,128)(2,1)} fusion(f32[1024,8192]{1,0:T(8,128)} %fusion.7, f32[1024,8192]{1,0:T(8,128)} %fusion.4, f32[1024,8192]{1,0:T(8,128)} %fusion.6, bf16[2,8192,256]{2,1,0:T(8,128)(2,1)} %reduce_sum.25, bf16[1,256,1024]{2,0,1:T(2,128)(2,1)S(1)} %get-tuple-element.14), kind=kOutput, calls=%fused_computation.8 | convolution fusion | flops 4328521728 | bytes 122159104 | tf_op jit(solution)/shard_map/dot_general | solution.py:22
  3321.9 23.0 pad_maximum_fusion
  (15 shorter events, 0.9 us)
Async XLA Ops:
  7.2 442.9 %all-gather.6.cloned.1.call-start = ((), (), s32[]{:S(2)}) async-start(), calls=%async_computation.1 | async-start | bytes 41943040 | tf_op jit(solution)/shard_map/all_gather | solution.py:39
  218.6 30.6 copy-start.1
  218.6 36.3 %copy-start.2 = (s32[4]{0:T(128)S(1)}, s32[4]{0:T(128)}, u32[]{:S(2)}) copy-start(s32[4]{0:T(128)} %param.6) | copy-start | bytes 52
  249.2 1638.0 %all-gather.10.cloned.1.call-start = ((), (), s32[]{:S(2)}) async-start(), calls=%async_computation.3 | async-start | bytes 75497472 | tf_op jit(solution)/shard_map/all_gather | solution.py:15
  620.2 2535.4 %all-gather.8.cloned.1.call-start = ((), (), s32[]{:S(2)}) async-start(), calls=%async_computation.2 | async-start | bytes 75497472 | tf_op jit(solution)/shard_map/all_gather | solution.py:15
  1915.8 18.9 copy-start
Sparse Core Ops, SparseCore 0:
  249.3 200.7 all-gather.5
  620.3 1266.7 all-gather.9
  1888.7 1266.8 all-gather.7
